TPU v7x, 32 devices: a whole 2x2x4 slice. The times are simulated.
32 devices in a mesh: ctx: 16 (over z, y, x), head: 2 (over core).
Axes of the slice: x: 2, y: 2, z: 4, core: 2. Of those that a mesh axis runs over, the one named last changes fastest.
Arguments:
- queries: bfloat16 [4096, 4096], P('ctx', 'head')
- keys: bfloat16 [4096, 1024], P('ctx', 'head')
- values: bfloat16 [4096, 1024], P('ctx', 'head'), may hold values from -6 to 6
- positions: int32 [4096], P('ctx'), may hold values from 0 to 6143, as said below
- retrieval: int32 [4], replicated, may hold values from 0 to 7, as said below
- yarn_scale: int32 [1], replicated, may hold values from 2 to 8
- out_weight: bfloat16 [4096, 4096], P('head', 'ctx'), may hold values from -0.125 to 0.125
Outputs:
- layer_out: bfloat16 [4096, 4096], P('ctx', 'head')
Inputs may be any that keep to these rules, and one draw needn't show every extreme that they name: positions start at 0 and rise by 1 or 2 from one token to the next, by 2 at exactly 2048 of the steps. `retrieval`: 4 different KV-head indices.
All inputs are finite; a program needn't handle non-finite values.
Results may differ from a plain program's by a relative error of at most 0.014.
The roundings to bfloat16 on the way count: a program that leaves them out, or rounds other values in their place, can miss the bound.
Values may be sent and summed in bfloat16 or wider, within the bound.
No kernel may reach another device: no remote copies, remote signals or barrier semaphores. Data moves between devices by JAX's collectives and lax.ppermute only.
A program may use at most 128 MiB of HBM per device.

v0:
```python
from functools import partial
import math
import jax
import jax.numpy as jnp
from jax import lax
from jax.sharding import PartitionSpec as P

HEAD_SIZE = 128
SINK = 64
WINDOW = 256
ORIG_CTX = 8192
QUERY_PER_KEY = 4
rope_base = 500000.0
neg_big = -1e30


def yarn_tables(positions, yarn_scale):
    half_size = HEAD_SIZE // 2
    factor = yarn_scale[0].astype(jnp.float32)
    freq_index = jnp.arange(half_size, dtype=jnp.float32)
    base_freq = jnp.power(jnp.float32(rope_base), -2.0 * freq_index / HEAD_SIZE)
    wave_ratio = ORIG_CTX * base_freq / (2.0 * math.pi)
    ramp_weight = jnp.clip((wave_ratio - 1.0) / 31.0, 0.0, 1.0)
    yarn_freq = base_freq * ramp_weight + base_freq / factor * (1.0 - ramp_weight)
    angles = positions.astype(jnp.float32)[:, None] * yarn_freq[None, :]
    mscale = 0.1 * jnp.log(factor) + 1.0
    return (jnp.cos(angles) * mscale, jnp.sin(angles) * mscale)


def apply_rotary(x, cosine_lookup, sine_lookup, head_count):
    row_count = x.shape[0]
    shaped = x.astype(jnp.float32).reshape(row_count, head_count, HEAD_SIZE)
    lower_half = shaped[..., : HEAD_SIZE // 2]
    upper_half = shaped[..., HEAD_SIZE // 2 :]
    cosine = cosine_lookup[:, None, :]
    sine_part = sine_lookup[:, None, :]
    rotated = jnp.concatenate(
        [
            lower_half * cosine - upper_half * sine_part,
            upper_half * cosine + lower_half * sine_part,
        ],
        axis=-1,
    )
    return rotated.reshape(row_count, head_count * HEAD_SIZE).astype(jnp.bfloat16)


def update(query_rows, key_block, value_block, visible, partial_state):
    row_max, totals, accum = partial_state
    scores = jnp.einsum(
        "rhgd,khd->hgrk", query_rows, key_block, preferred_element_type=jnp.float32
    ) * (1.0 / math.sqrt(HEAD_SIZE))
    mask_full = visible[:, None]
    scores = jnp.where(mask_full, scores, neg_big)
    new_max = jnp.maximum(row_max, jnp.max(scores, axis=-1))
    weights = jnp.where(mask_full, jnp.exp(scores - new_max[..., None]), 0.0)
    rescale = jnp.exp(row_max - new_max)
    totals = totals * rescale + jnp.sum(weights, axis=-1)
    accum = accum * rescale[..., None] + jnp.einsum(
        "hgrk,khd->hgrd",
        weights.astype(jnp.bfloat16),
        value_block,
        preferred_element_type=jnp.float32,
    )
    return (new_max, totals, accum)


def attend(query_sets, rotated_key, values, flags, kv_local):
    shaped_sets = []
    initial = []
    for query_rows, query_index in query_sets:
        row_count = query_rows.shape[0]
        shaped_sets.append(
            (query_rows.reshape(row_count, kv_local, QUERY_PER_KEY, HEAD_SIZE), query_index)
        )
        initial.append(
            (
                jnp.full((kv_local, QUERY_PER_KEY, row_count), neg_big, jnp.float32),
                jnp.zeros((kv_local, QUERY_PER_KEY, row_count), jnp.float32),
                jnp.zeros((kv_local, QUERY_PER_KEY, row_count, HEAD_SIZE), jnp.float32),
            )
        )
    initial = tuple(initial)
    key_shard = lax.all_gather(rotated_key, "ctx", axis=0, tiled=True)
    value_shard = lax.all_gather(values, "ctx", axis=0, tiled=True)
    shard_rows = key_shard.shape[0]
    sub_rows = math.gcd(shard_rows, 512)
    turn_count = shard_rows // sub_rows

    def one_turn(j, inner_states):
        key_block = lax.dynamic_slice_in_dim(key_shard, j * sub_rows, sub_rows, 0).reshape(
            sub_rows, kv_local, HEAD_SIZE
        )
        value_block = lax.dynamic_slice_in_dim(value_shard, j * sub_rows, sub_rows, 0).reshape(
            sub_rows, kv_local, HEAD_SIZE
        )
        key_index = j * sub_rows + jnp.arange(sub_rows, dtype=jnp.int32)
        updated = []
        for (query_rows, query_index), partial_state in zip(shaped_sets, inner_states):
            causal = key_index[None, :] <= query_index[:, None]
            nearby = (key_index[None, :] < SINK) | (
                key_index[None, :] > query_index[:, None] - WINDOW
            )
            visible = causal[None] & (flags[:, None, None] | nearby[None])
            updated.append(
                lax.cond(
                    jnp.any(visible),
                    partial(update, query_rows, key_block, value_block, visible),
                    lambda keep_state: keep_state,
                    partial_state,
                )
            )
        return tuple(updated)

    final = lax.fori_loop(0, turn_count, one_turn, initial)
    results = []
    for (query_rows, query_index), (row_max, totals, accum) in zip(shaped_sets, final):
        output = accum / totals[..., None]
        results.append(
            output.transpose(2, 0, 1, 3)
            .reshape(query_rows.shape[0], kv_local * QUERY_PER_KEY * HEAD_SIZE)
            .astype(jnp.bfloat16)
        )
    return results


def shards(queries, keys, values, positions, retrieval, yarn_scale, out_weight):
    rows_dev = queries.shape[0]
    kv_local = keys.shape[1] // HEAD_SIZE
    cosine_lookup, sine_lookup = yarn_tables(positions, yarn_scale)
    rotated_query = apply_rotary(queries, cosine_lookup, sine_lookup, kv_local * QUERY_PER_KEY)
    rotated_key = apply_rotary(keys, cosine_lookup, sine_lookup, kv_local)
    ctx_index = lax.axis_index("ctx")
    head_ids = lax.axis_index("head") * kv_local + jnp.arange(kv_local, dtype=jnp.int32)
    flags = jnp.any(head_ids[:, None] == retrieval[None, :], axis=1)
    own_index = ctx_index * rows_dev + jnp.arange(rows_dev, dtype=jnp.int32)
    attended = attend(((rotated_query, own_index),), rotated_key, values, flags, kv_local)[0]
    partials = jnp.dot(
        attended,
        lax.all_gather(out_weight, "ctx", axis=1, tiled=True),
        preferred_element_type=jnp.float32,
    )
    return lax.psum_scatter(partials.astype(jnp.bfloat16), "head", scatter_dimension=1, tiled=True)


def solution(mesh):
    return jax.shard_map(
        shards,
        mesh=mesh,
        in_specs=(
            P("ctx", "head"),
            P("ctx", "head"),
            P("ctx", "head"),
            P("ctx"),
            P(),
            P(),
            P("head", "ctx"),
        ),
        out_specs=P("ctx", "head"),
        check_vma=False,
    )
```

profile of v0, /device:TPU:0, one launch (start us, length us, event | category | flops | bytes accessed | tf_op | source)
XLA Modules:
  0.0 449.2 jit_solution(7395130143101550300)
XLA Ops:
  7.3 1.1 copy.51
  14.0 1.4 subtract_convert_fusion
  16.0 84.0 %all-gather.4.cloned.1.call-done = bf16[4096,512]{0,1:T(8,128)(2,1)} async-done(((bf16[256,512]{0,1:T(8,128)(2,1)}), bf16[4096,512]{0,1:T(8,128)(2,1)}) %all-gather.4.cloned.1.call-update) | async-done | bytes 4194320 | tf_op jit(solution)/shard_map/all_gather | solution.py:83
  100.0 87.7 %all-gather.6.cloned.1.call-done = bf16[4096,512]{0,1:T(8,128)(2,1)} async-done(((bf16[256,512]{0,1:T(8,128)(2,1)}), bf16[4096,512]{0,1:T(8,128)(2,1)}) %all-gather.6.cloned.1.call-update) | async-done | bytes 4194320 | tf_op jit(solution)/shard_map/all_gather | solution.py:84
  187.7 1.6 broadcast_in_dim.68
  189.3 29.0 %while.20 = (s32[]{:T(128)}, f32[4,4,256]{2,1,0:T(4,128)S(1)}, f32[4,4,256]{2,1,0:T(4,128)S(1)}, f32[4,4,256,128]{3,2,1,0:T(8,128)}, pred[4]{0:T(512)(128)(4,1)S...) while((s32[]{:T(128)}, f32[4,4,256]{2,1,0:T(4,128)S(1)}, ...), condition=%wide.region_7.8_spmd.clone, body=%wide.region_1.7_spmd.clone.sunk | while | flops 1104029696 | bytes 53224808 | solution.py:114
  189.5 1.4 fusion.24
  191.5 10.4 %conditional.3 = ((f32[4,4,256]{2,1,0:T(4,128)S(1)}, f32[4,4,256]{2,1,0:T(4,128)S(1)}, f32[4,4,256,128]{3,2,1,0:T(8,128)})) conditional(s32[]{:T(128)} %convert_element_type.65, (f32[4,4,256]{2,1,0:T(4,128)S(1)}, f32[4,4,256]{2,1,0:T(4,128)S(1)}, f32[4,4,256,128]{3,2,1,0:T(8,128)}) %tuple.78, (pred[4,256,512]{1,2,0:T(8,128)(4,1)S(1)}, s32[]{:T(128)}, ...), branch_computations={%region_3.3_spmd, %region_4.6_spmd} | conditional | flops 1102061568 | bytes 52166780 | solution.py:105
  191.6 1.3 constant_dynamic-slice_fusion
  192.8 1.9 fusion.2
  194.8 2.1 fusion.4
  196.9 3.6 multiply_add_fusion
  200.6 1.4 copy-done.1
  202.2 1.4 fusion.24
  204.5 1.4 fusion.24
  206.9 1.4 fusion.24
  209.2 1.4 fusion.24
  211.5 1.4 fusion.24
  213.9 1.4 fusion.24
  216.2 1.4 fusion.24
  218.3 1.9 copy.43
  220.4 202.8 %all-gather.8.cloned.1.call-done = bf16[2048,4096]{1,0:T(8,128)(2,1)} async-done(((bf16[2048,256]{1,0:T(8,128)(2,1)}), bf16[2048,4096]{1,0:T(8,128)(2,1)}) %all-gather.8.cloned.1.call-update) | async-done | bytes 16777232 | tf_op jit(solution)/shard_map/all_gather | solution.py:139
  423.2 11.5 %convolution_convert_fusion = bf16[256,4096]{1,0:T(8,128)(2,1)} fusion(bf16[256,2048]{0,1:T(8,128)(2,1)S(1)} %bitcast.49, bf16[2048,4096]{1,0:T(8,128)(2,1)} %all-gather.8.cloned.1.call-done), kind=kOutput, calls=%fused_computation.23 | convolution fusion | flops 4296015872 | bytes 19922944 | tf_op jit(solution)/shard_map/dot_general | solution.py:137
  434.7 8.0 %reduce-scatter.2.cloned.1.call-done = bf16[256,2048]{1,0:T(8,128)(2,1)} async-done(((bf16[256,4096]{1,0:T(8,128)(2,1)}), bf16[256,2048]{1,0:T(8,128)(2,1)}) %reduce-scatter.2.cloned.1.call-update) | async-done | bytes 1048592 | tf_op jit(solution)/shard_map/reduce_scatter | solution.py:142
  (76 shorter events, 8.4 us)
Async XLA Ops:
  6.5 3.8 copy-start.3
  6.5 93.4 %all-gather.4.cloned.1.call-start = ((), (), s32[]{:S(2)}) async-start(), calls=%async_computation.1 | async-start | bytes 4456448 | tf_op jit(solution)/shard_map/all_gather | solution.py:83
  8.4 3.8 copy-start.2
  10.3 177.4 %all-gather.6.cloned.1.call-start = ((), (), s32[]{:S(2)}) async-start(), calls=%async_computation.2 | async-start | bytes 4456448 | tf_op jit(solution)/shard_map/all_gather | solution.py:84
  11.2 411.9 %all-gather.8.cloned.1.call-start = ((), (), s32[]{:S(2)}) async-start(), calls=%async_computation.3 | async-start | bytes 17825792 | tf_op jit(solution)/shard_map/all_gather | solution.py:139
  12.0 430.7 %reduce-scatter.2.cloned.1.call-start = ((), (), s32[]{:S(2)}) async-start(), calls=%async_computation.4 | async-start | bytes 3145728 | tf_op jit(solution)/shard_map/reduce_scatter | solution.py:142
  12.5 0.7 copy-start.4
  194.7 2.2 copy-start
  200.6 1.4 copy-start.1
Sparse Core Ops, SparseCore 0:
  10.4 89.4 all-gather.3
  102.7 84.9 all-gather.5
  190.4 232.7 all-gather.7
  434.8 7.8 reduce-scatter.1
where the time goes:
time: 450 us; the launch traced here: 449 us
  waiting for transfers between devices  383 us (85%)
  other arithmetic  19.6 us (4%)
  matrix products  17 us (4%)
  between operations  14 us (3%)
  local copies, waits for them, and re-layouts  9.6 us (2%)
  loops' own time  5.67 us (1%)
    all_gather x1, waiting for transfers between devices, shards(): lax.all_gather(out_weight, 'ctx', axis=1, tiled=True)  203 us
    all_gather x1, waiting for transfers between devices, attend(): value_shard = lax.all_gather(values, 'ctx', axis=0, tiled=True)  87.7 us
    all_gather x1, waiting for transfers between devices, attend(): key_shard = lax.all_gather(rotated_key, 'ctx', axis=0, tiled=True)  84 us
    dot_general x1, matrix products, shards(): jnp.dot(attended, lax.all_gather(out_weight, 'ctx', axis=1, tiled=True),...  11.5 us
    reduce_or x8, other arithmetic, one_turn(): jnp.any(visible)  11.1 us
  transfers between devices with their start and end apart: 4, of which 4 were waited for; matrix products, arithmetic and copies ran while one was open for 7% of the time, Pallas kernels for 0%

commit v1 on v0

--- a/solution.py
+++ b/solution.py
@@ -80,8 +80,11 @@
             )
         )
     initial = tuple(initial)
-    key_shard = lax.all_gather(rotated_key, "ctx", axis=0, tiled=True)
-    value_shard = lax.all_gather(values, "ctx", axis=0, tiled=True)
+    key_shard, value_shard = jnp.split(
+        lax.all_gather(jnp.concatenate([rotated_key, values], axis=1), "ctx", axis=0, tiled=True),
+        [rotated_key.shape[1]],
+        axis=1,
+    )
     shard_rows = key_shard.shape[0]
     sub_rows = math.gcd(shard_rows, 512)
     turn_count = shard_rows // sub_rows

time: 450 us -> 411 us (0.913)
  waiting for transfers between devices: 383 us -> 338 us
  local copies, waits for them, and re-layouts: 9.6 us -> 15.7 us
    all_gather x2 -> x1, waiting for transfers between devices: 172 us -> 133 us  [attend(): lax.all_gather(jnp.concatenate([rotated_key, values], axis=1), 'ctx', axi...]
    split x0 -> x1, local copies, waits for them, and re-layouts: none -> 5.93 us  [attend(): jnp.split(lax.all_gather(jnp.concatenate([rotated_key, values], axis=1),...]
    all_gather x1, waiting for transfers between devices: 203 us -> 197 us  [shards(): lax.all_gather(out_weight, 'ctx', axis=1, tiled=True)]
  transfers between devices with their start and end apart: 4 -> 3, of which waited for: 4 -> 3; matrix products, arithmetic and copies ran while one was open for 7% -> 9% of each run, Pallas kernels for 0% -> 0%
where the time goes in v1:
time: 411 us; the launch traced here: 410 us
  waiting for transfers between devices  338 us (82%)
  other arithmetic  19.6 us (5%)
  matrix products  17 us (4%)
  local copies, waits for them, and re-layouts  15.7 us (4%)
  between operations  14 us (3%)
  loops' own time  5.6 us (1%)
    all_gather x1, waiting for transfers between devices, shards(): lax.all_gather(out_weight, 'ctx', axis=1, tiled=True)  197 us
    all_gather x1, waiting for transfers between devices, attend(): lax.all_gather(jnp.concatenate([rotated_key, values], axis=1), 'ctx', axi...  133 us
    dot_general x1, matrix products, shards(): jnp.dot(attended, lax.all_gather(out_weight, 'ctx', axis=1, tiled=True),...  11.5 us
    reduce_or x8, other arithmetic, one_turn(): jnp.any(visible)  11 us
  transfers between devices with their start and end apart: 3, of which 3 were waited for; matrix products, arithmetic and copies ran while one was open for 9% of the time, Pallas kernels for 0%

profile of v1, /device:TPU:0, one launch (start us, length us, event | category | flops | bytes accessed | tf_op | source)
XLA Modules:
  0.0 410.3 jit_solution(7857224588594974255)
XLA Ops:
  7.2 1.1 copy.27
  14.2 1.4 subtract_convert_fusion
  16.1 132.6 %all-gather.3.cloned.1.call-done = bf16[4096,1024]{0,1:T(8,128)(2,1)} async-done(((bf16[256,1024]{0,1:T(8,128)(2,1)}), bf16[4096,1024]{0,1:T(8,128)(2,1)}) %all-gather.3.cloned.1.call-update) | async-done | bytes 8388624 | tf_op jit(solution)/shard_map/all_gather | solution.py:84
  148.8 5.9 %fusion.17 = (bf16[4096,512]{0,1:T(8,128)(2,1)}, bf16[4096,512]{0,1:T(8,128)(2,1)}) fusion(bf16[4096,1024]{0,1:T(8,128)(2,1)} %all-gather.3.cloned.1.call-done), kind=kLoop, calls=%fused_computation.42 | loop fusion | bytes 16777216 | tf_op jit(solution)/shard_map/split | solution.py:83
  154.7 1.5 broadcast_in_dim.68
  156.3 28.9 %while.20 = (s32[]{:T(128)}, f32[4,4,256]{2,1,0:T(4,128)S(1)}, f32[4,4,256]{2,1,0:T(4,128)S(1)}, f32[4,4,256,128]{3,2,1,0:T(8,128)}, pred[4]{0:T(512)(128)(4,1)S...) while((s32[]{:T(128)}, f32[4,4,256]{2,1,0:T(4,128)S(1)}, ...), condition=%wide.region_7.8_spmd.clone, body=%wide.region_1.7_spmd.clone.sunk | while | flops 1104029696 | bytes 53224808 | solution.py:117
  156.5 1.4 fusion.25
  158.5 10.4 %conditional.3 = ((f32[4,4,256]{2,1,0:T(4,128)S(1)}, f32[4,4,256]{2,1,0:T(4,128)S(1)}, f32[4,4,256,128]{3,2,1,0:T(8,128)})) conditional(s32[]{:T(128)} %convert_element_type.65, (f32[4,4,256]{2,1,0:T(4,128)S(1)}, f32[4,4,256]{2,1,0:T(4,128)S(1)}, f32[4,4,256,128]{3,2,1,0:T(8,128)}) %tuple.79, (pred[4,256,512]{1,2,0:T(8,128)(4,1)S(1)}, s32[]{:T(128)}, ...), branch_computations={%region_3.3_spmd, %region_4.6_spmd} | conditional | flops 1102061568 | bytes 52166780 | solution.py:108
  158.5 1.4 constant_dynamic-slice_fusion
  159.9 1.9 fusion.2
  161.8 2.1 fusion.4
  164.0 3.6 multiply_add_fusion
  167.6 1.3 copy-done.1
  169.2 1.4 fusion.25
  171.5 1.4 fusion.25
  173.8 1.4 fusion.25
  176.1 1.4 fusion.25
  178.5 1.4 fusion.25
  180.8 1.4 fusion.25
  183.1 1.4 fusion.25
  185.1 1.9 copy.32
  187.3 197.0 %all-gather.5.cloned.1.call-done = bf16[2048,4096]{1,0:T(8,128)(2,1)} async-done(((bf16[2048,256]{1,0:T(8,128)(2,1)}), bf16[2048,4096]{1,0:T(8,128)(2,1)}) %all-gather.5.cloned.1.call-update) | async-done | bytes 16777232 | tf_op jit(solution)/shard_map/all_gather | solution.py:142
  384.3 11.5 %convolution_convert_fusion = bf16[256,4096]{1,0:T(8,128)(2,1)} fusion(bf16[256,2048]{0,1:T(8,128)(2,1)S(1)} %bitcast.49, bf16[2048,4096]{1,0:T(8,128)(2,1)} %all-gather.5.cloned.1.call-done), kind=kOutput, calls=%fused_computation.23 | convolution fusion | flops 4296015872 | bytes 19922944 | tf_op jit(solution)/shard_map/dot_general | solution.py:140
  395.8 8.0 %reduce-scatter.2.cloned.1.call-done = bf16[256,2048]{1,0:T(8,128)(2,1)} async-done(((bf16[256,4096]{1,0:T(8,128)(2,1)}), bf16[256,2048]{1,0:T(8,128)(2,1)}) %reduce-scatter.2.cloned.1.call-update) | async-done | bytes 1048592 | tf_op jit(solution)/shard_map/reduce_scatter | solution.py:145
  (73 shorter events, 8.6 us)
Async XLA Ops:
  6.5 142.2 %all-gather.3.cloned.1.call-start = ((), (), s32[]{:S(2)}) async-start(), calls=%async_computation.1 | async-start | bytes 8912896 | tf_op jit(solution)/shard_map/all_gather | solution.py:84
  10.4 2.0 copy-start.2
  11.4 372.9 %all-gather.5.cloned.1.call-start = ((), (), s32[]{:S(2)}) async-start(), calls=%async_computation.2 | async-start | bytes 17825792 | tf_op jit(solution)/shard_map/all_gather | solution.py:142
  12.2 391.6 %reduce-scatter.2.cloned.1.call-start = ((), (), s32[]{:S(2)}) async-start(), calls=%async_computation.3 | async-start | bytes 3145728 | tf_op jit(solution)/shard_map/reduce_scatter | solution.py:145
  12.7 0.7 copy-start.3
  161.8 2.2 copy-start
  167.6 1.3 copy-start.1
Sparse Core Ops, SparseCore 0:
  11.5 137.1 all-gather.2
  151.5 232.7 all-gather.4
  395.9 7.7 reduce-scatter.1
